TPU v7x, 512 devices: a whole 4x8x8 slice. The times are simulated.
512 devices in a mesh: space: 64 (over x, y, core), chan: 8 (over z).
Axes of the slice: x: 4, y: 8, z: 8, core: 2. Of those that a mesh axis runs over, the one named last changes fastest.
Arguments:
- features: bfloat16 [128, 64, 4096], P('space', 'chan'), may hold values from -6 to 6
- conv_weight: bfloat16 [128, 9, 64], P('chan'), may hold values from -0.25 to 0.25
- down_weight: bfloat16 [128, 4, 128], P('chan'), may hold values from -0.25 to 0.25
- cotangent: bfloat16 [128, 128, 1024], P('space', 'chan'), may hold values from -16 to 16
- partner: int32 [128, 4], P('space'), may hold values from 0 to 511, as said below
- orientation: int32 [128, 4], P('space'), may hold values from 0 to 1, as said below
Outputs:
- pooled: bfloat16 [128, 128, 1024], P('space', 'chan')
- features_grad: bfloat16 [128, 64, 4096], P('space', 'chan')
- conv_grad: float32 [128, 9, 64], P('chan')
- down_grad: float32 [128, 4, 128], P('chan')
Inputs may be any that keep to these rules, and one draw needn't show every extreme that they name: Bordering is mutual: the slot at partner[t, e] has partner 4 t + e; no edge borders itself; every slot 0 to 511 appears exactly once. `orientation`: both edges of a bordering pair carry the same value.
All inputs are finite; a program needn't handle non-finite values.
Results may differ from a plain program's by a relative error of at most 0.0049.
Values may be sent and summed in bfloat16 or wider, within the bound.
No kernel may reach another device: no remote copies, remote signals or barrier semaphores. Data moves between devices by JAX's collectives and lax.ppermute only.
A program may use at most 64 MiB of HBM per device.

v0:
```python
import jax
import jax.numpy as jnp
from jax import lax
from jax.sharding import PartitionSpec as P

S = 64


def edge_strips(values):
    return jnp.stack(
        [values[..., 0, :], values[..., :, -1], values[..., -1, :], values[..., :, 0]], axis=-3
    )


def rim_strips(padded):
    return jnp.stack(
        [padded[..., 0, 1:-1], padded[..., 1:-1, -1], padded[..., -1, 1:-1], padded[..., 1:-1, 0]],
        axis=-3,
    )


def bordering(strips, partner, orientation):
    flat = strips.reshape((-1,) + strips.shape[2:])
    picked = jnp.take(flat, partner.reshape(-1), axis=0)
    picked = picked.reshape(partner.shape + strips.shape[2:])
    return jnp.where((orientation == 1)[..., None, None], picked[..., ::-1], picked)


def pad_tile(values, halo_strips):
    tile_side = values.shape[-1]
    widths = [(0, 0)] * (values.ndim - 2) + [(1, 1), (1, 1)]
    padded = jnp.pad(values, widths)
    padded = padded.at[..., 0, 1 : tile_side + 1].set(halo_strips[..., 0, :, :])
    padded = padded.at[..., 1 : tile_side + 1, tile_side + 1].set(halo_strips[..., 1, :, :])
    padded = padded.at[..., tile_side + 1, 1 : tile_side + 1].set(halo_strips[..., 2, :, :])
    return padded.at[..., 1 : tile_side + 1, 0].set(halo_strips[..., 3, :, :])


def add_edges(interior, returned):
    interior = interior.at[..., 0, :].add(returned[..., 0, :, :])
    interior = interior.at[..., :, -1].add(returned[..., 1, :, :])
    interior = interior.at[..., -1, :].add(returned[..., 2, :, :])
    return interior.at[..., :, 0].add(returned[..., 3, :, :])


def unfold(padded, height, width):
    taps = [
        padded[..., row_shift : row_shift + height, col_shift : col_shift + width]
        for row_shift in range(3)
        for col_shift in range(3)
    ]
    return jnp.stack(taps, axis=-4)


def fold_taps(taps):
    total = None
    for row_shift in range(3):
        for col_shift in range(3):
            piece = taps[..., 3 * row_shift + col_shift, :, :, :]
            widths = [(0, 0)] * (piece.ndim - 2) + [
                (row_shift, 2 - row_shift),
                (col_shift, 2 - col_shift),
            ]
            placed = jnp.pad(piece, widths)
            total = placed if total is None else total + placed
    return total


def silu_grad(values):
    gate = jax.nn.sigmoid(values)
    return gate * (1.0 + values * (1.0 - gate))


def shards(features, conv_weight, down_weight, cotangent, partner, orientation):
    tile_count = features.shape[0]
    tile_side = S
    chan_count = lax.axis_size("chan")
    chan_index = lax.axis_index("chan")
    chan_part = features.shape[1]
    block_rows = tile_side // chan_count
    whole_features = lax.all_gather(features, "chan", axis=1, tiled=True)
    in_channels = whole_features.shape[1]
    images = whole_features.reshape(tile_count, in_channels, tile_side, tile_side)
    gathered = lax.all_gather(edge_strips(images), "space", axis=0, tiled=True)
    halo_strips = bordering(gathered, partner, orientation)
    padded = pad_tile(images, halo_strips)
    block = lax.dynamic_slice_in_dim(padded, chan_index * block_rows, block_rows + 2, 2)
    conv_full, down_full = (
        lax.all_gather(conv_weight, "chan", axis=0, tiled=True),
        lax.all_gather(down_weight, "chan", axis=0, tiled=True),
    )
    out_channels = conv_full.shape[0]
    columns = unfold(block, block_rows, tile_side)
    pre_act = jnp.einsum("okc,tkcrs->tors", conv_full, columns, preferred_element_type=jnp.float32)
    activated = jax.nn.silu(pre_act).astype(jnp.bfloat16)
    quads = activated.reshape(tile_count, out_channels, block_rows // 2, 2, tile_side // 2, 2)
    down_taps = down_full.reshape(out_channels, 2, 2, out_channels)
    pooled_rows = jnp.einsum(
        "opqc,tcipjq->toij", down_taps, quads, preferred_element_type=jnp.float32
    ).astype(jnp.bfloat16)
    pooled_band = pooled_rows.reshape(tile_count, out_channels, block_rows // 2 * (tile_side // 2))
    pooled = lax.all_to_all(pooled_band, "chan", split_axis=1, concat_axis=2, tiled=True)
    grad_flat = lax.all_to_all(cotangent, "chan", split_axis=2, concat_axis=1, tiled=True)
    grad_band = grad_flat.reshape(tile_count, out_channels, block_rows // 2, tile_side // 2)
    down_part = jnp.einsum(
        "toij,tcipjq->opqc", grad_band, quads, preferred_element_type=jnp.float32
    )
    down_part = down_part.reshape(out_channels, 4, out_channels)
    grad_act = jnp.einsum(
        "opqc,toij->tcipjq", down_taps, grad_band, preferred_element_type=jnp.float32
    )
    grad_act = grad_act.reshape(tile_count, out_channels, block_rows, tile_side)
    grad_pre = (grad_act * silu_grad(pre_act)).astype(jnp.bfloat16)
    conv_part = jnp.einsum("tors,tkcrs->okc", grad_pre, columns, preferred_element_type=jnp.float32)
    grad_block = fold_taps(
        jnp.einsum("okc,tors->tkcrs", conv_full, grad_pre, preferred_element_type=jnp.float32)
    )
    row_blocks = lax.all_to_all(
        grad_block[None].astype(jnp.bfloat16), "chan", split_axis=2, concat_axis=0, tiled=True
    ).astype(jnp.float32)
    stacked = jnp.moveaxis(row_blocks, 0, 2)
    inner = stacked[:, :, :, 1 : block_rows + 1, :].reshape(
        tile_count, chan_part, tile_side, tile_side + 2
    )
    grad_padded = jnp.pad(inner, ((0, 0), (0, 0), (1, 1), (0, 0)))
    grad_padded = grad_padded.at[:, :, 0:tile_side:block_rows, :].add(stacked[:, :, :, 0, :])
    grad_padded = grad_padded.at[:, :, block_rows + 1 : tile_side + 2 : block_rows, :].add(
        stacked[:, :, :, block_rows + 1, :]
    )
    rim_all = lax.all_gather(rim_strips(grad_padded), "space", axis=0, tiled=True)
    returned = bordering(rim_all, partner, orientation)
    features_grad = add_edges(grad_padded[:, :, 1:-1, 1:-1], returned).astype(jnp.bfloat16)
    features_grad = features_grad.reshape(tile_count, chan_part, tile_side * tile_side)
    grad_scale = float(lax.axis_size("space") * tile_count * tile_side * tile_side) ** (-0.5)
    share = out_channels // chan_count
    conv_total, down_total = lax.psum((conv_part, down_part), ("space", "chan"))
    conv_grad = lax.dynamic_slice_in_dim(conv_total, chan_index * share, share, 0)
    down_grad = lax.dynamic_slice_in_dim(down_total, chan_index * share, share, 0)
    return (pooled, features_grad, conv_grad * grad_scale, down_grad * grad_scale)


def solution(mesh):
    placed = (
        P("space", "chan", None),
        P("chan", None, None),
        P("chan", None, None),
        P("space", "chan", None),
        P("space", None),
        P("space", None),
    )
    return jax.shard_map(
        shards,
        mesh=mesh,
        in_specs=placed,
        out_specs=(
            P("space", "chan", None),
            P("space", "chan", None),
            P("chan", None, None),
            P("chan", None, None),
        ),
        check_vma=False,
    )
```

profile of v0, /device:TPU:1, one launch (start us, length us, event | category | flops | bytes accessed | tf_op | source)
XLA Modules:
  0.0 560.8 jit_solution(13366105239182730253)
XLA Ops:
  8.0 44.8 %all-gather.4.cloned.1.call-done = bf16[2,64,4096]{2,1,0:T(8,128)(2,1)} async-done(((bf16[2,8,4096]{2,1,0:T(8,128)(2,1)}), bf16[2,64,4096]{2,1,0:T(8,128)(2,1)}) %all-gather.4.cloned.1.call-update) | async-done | bytes 1048592 | tf_op jit(solution)/shard_map/all_gather | solution.py:81
  52.8 2.0 copy.217
  57.6 4.4 all-to-all-start.1
  62.1 20.6 %all_gather.17 = bf16[128,9,64]{2,0,1:T(8,128)(2,1)S(1)} all-gather(bf16[16,9,64]{2,0,1:T(8,128)(2,1)S(1)} %copy-done.7), channel_id=1, replica_groups=mesh['space'=64,'chan'=8] {'chan'}, dimensions={0}, use_global_device_ids=true | all-gather | bytes 165888 | tf_op jit(solution)/shard_map/all_gather | solution.py:89
  82.8 18.9 %all_gather.18 = bf16[128,4,128]{2,1,0:T(4,128)(2,1)S(1)} all-gather(bf16[16,4,128]{2,1,0:T(4,128)(2,1)S(1)} %copy-done.8), channel_id=1, replica_groups=mesh['space'=64,'chan'=8] {'chan'}, dimensions={0}, use_global_device_ids=true | all-gather | bytes 147456 | tf_op jit(solution)/shard_map/all_gather | solution.py:90
  104.8 2.6 pad.68
  107.4 40.1 %all-gather.6.cloned.1.call-done = bf16[128,4,64,64]{2,3,0,1:T(8,128)(2,1)} async-done(((bf16[2,4,64,64]{2,3,0,1:T(8,128)(2,1)}), bf16[128,4,64,64]{2,3,0,1:T(8,128)(2,1)}) %all-gather.6.cloned.1.call-update) | async-done | bytes 4194320 | tf_op jit(solution)/shard_map/all_gather | solution.py:84
  147.5 11.9 %copy.224 = bf16[128,4,64,64]{3,2,1,0:T(8,128)(2,1)} copy(bf16[128,4,64,64]{2,3,0,1:T(8,128)(2,1)} %all-gather.6.cloned.1.call-done) | data formatting | bytes 8388608 | tf_op jit(solution)/shard_map/all_gather | solution.py:84
  159.4 4.0 gather_fusion
  163.9 1.5 scatter.14
  165.4 1.4 scatter.15
  169.6 1.6 multiply_convert_fusion
  174.7 7.1 %all-to-all-start.2 = ((bf16[1,2,64,10,66]{4,1,3,0,2:T(2,128)(2,1)}), bf16[1,2,64,10,66]{4,1,3,0,2:T(2,128)(2,1)S(1)}, u32[]{:S(2)}, u32[]{:S(2)}) async-start(bf16[1,2,64,10,66]{4,1,3,0,2:T(2,128)(2,1)} %copy.255), calls=%async_computation.2 | async-start | bytes 655360 | tf_op jit(solution)/shard_map/all_to_all | solution.py:118
  181.8 2.2 fusion.15
  184.0 1.8 copy.272
  187.4 8.1 %all-to-all-done.2 = bf16[1,2,64,10,66]{4,1,3,0,2:T(2,128)(2,1)S(1)} async-done(((bf16[1,2,64,10,66]{4,1,3,0,2:T(2,128)(2,1)}), bf16[1,2,64,10,66]{4,1,3,0,2:T(2,128)(2,1)S(1)}, u32[]{:S(2)}, u32[]{:S(2)}) %all-to-all-start.2) | async-done | bytes 168992 | tf_op jit(solution)/shard_map/all_to_all | solution.py:118
  199.9 3.4 all-to-all-start
  203.3 7.1 %all-to-all-done = bf16[2,128,128]{2,0,1:T(2,128)(2,1)S(1)} async-done(((bf16[2,128,128]{2,0,1:T(2,128)(2,1)}), bf16[2,128,128]{2,0,1:T(2,128)(2,1)S(1)}, u32[]{:S(2)}, u32[]{:S(2)}) %all-to-all-start) | async-done | bytes 65568 | tf_op jit(solution)/shard_map/all_to_all | solution.py:102
  211.1 248.5 %all-reduce.14.cloned.1.call-done = (f32[128,9,64]{2,0,1:T(8,128)}, f32[128,4,128]{2,1,0:T(4,128)}) async-done(((f32[128,9,64]{2,0,1:T(8,128)}, f32[128,4,128]{2,1,0:T(4,128)}), (f32[128,9,64]{2,0,1:T(8,128)}, f32[128,4,128]{2,1,0:T(4,128)})) %all-reduce.14.cloned.1.call-update) | async-done | bytes 557072 | tf_op jit(solution)/shard_map/psum | solution.py:136
  461.0 1.5 dynamic-slice_multiply_fusion
  463.0 74.2 %all-gather.8.cloned.1.call-done = f32[128,4,8,64]{3,2,0,1:T(8,128)} async-done(((f32[2,4,8,64]{3,2,0,1:T(8,128)}), f32[128,4,8,64]{3,2,0,1:T(8,128)}) %all-gather.8.cloned.1.call-update) | async-done | bytes 1048592 | tf_op jit(solution)/shard_map/all_gather | solution.py:130
  537.2 1.9 copy.264
  540.3 1.8 scatter-add.36
  542.6 10.4 %scatter-add.38 = f32[2,8,64,64]{2,1,0,3:T(8,128)S(1)} dynamic-update-slice(f32[2,8,64,64]{2,1,0,3:T(8,128)S(1)} %fusion.23, f32[2,8,1,64]{2,1,0,3:T(8,128)S(1)} %slice_add_fusion, s32[]{:T(128)} %constant.268.clone.1, s32[]{:T(128)} %constant.268.clone.1, s32[]{:T(128)} %constant.280.clone.1, s32[]{:T(128)} %constant.268.clone.1) | dynamic-update-slice | bytes 8196 | tf_op jit(solution)/shard_map/scatter-add | solution.py:42
  (112 shorter events, 24.8 us)
Async XLA Ops:
  7.2 48.9 %copy-start.6 = (bf16[2,16,1024]{2,1,0:T(8,128)(2,1)S(1)}, bf16[2,16,1024]{2,1,0:T(8,128)(2,1)}, u32[]{:S(2)}) copy-start(bf16[2,16,1024]{2,1,0:T(8,128)(2,1)} %param.25) | copy-start | bytes 196612
  7.2 45.7 %all-gather.4.cloned.1.call-start = ((), (), s32[]{:S(2)}) async-start(), calls=%async_computation.3 | async-start | bytes 1179648 | tf_op jit(solution)/shard_map/all_gather | solution.py:81
  7.9 54.1 %copy-start.9 = (s32[2,4]{1,0:T(2,128)S(1)}, s32[2,4]{1,0:T(2,128)}, u32[]{:S(2)}) copy-start(s32[2,4]{1,0:T(2,128)} %param.26) | copy-start | bytes 100
  7.9 54.2 %copy-start.7 = (bf16[16,9,64]{2,0,1:T(8,128)(2,1)S(1)}, bf16[16,9,64]{2,0,1:T(8,128)(2,1)}, u32[]{:S(2)}) copy-start(bf16[16,9,64]{2,0,1:T(8,128)(2,1)} %param.23) | copy-start | bytes 55300
  7.9 74.8 %copy-start.10 = (s32[2,4]{1,0:T(2,128)S(1)}, s32[2,4]{1,0:T(2,128)}, u32[]{:S(2)}) copy-start(s32[2,4]{1,0:T(2,128)} %param.27) | copy-start | bytes 100
  7.9 74.8 %copy-start.8 = (bf16[16,4,128]{2,1,0:T(4,128)(2,1)S(1)}, bf16[16,4,128]{2,1,0:T(4,128)(2,1)}, u32[]{:S(2)}) copy-start(bf16[16,4,128]{2,1,0:T(4,128)(2,1)} %param.24) | copy-start | bytes 49156
  8.0 139.6 %all-gather.6.cloned.1.call-start = ((), (), s32[]{:S(2)}) async-start(), calls=%async_computation.4 | async-start | bytes 8519680 | tf_op jit(solution)/shard_map/all_gather | solution.py:84
  54.9 48.7 %copy-start = (bf16[2,64,4096]{1,2,0:T(8,128)(2,1)}, bf16[2,64,4096]{1,2,0:T(8,128)(2,1)S(1)}, u32[]{:S(2)}) copy-start(bf16[2,64,4096]{1,2,0:T(8,128)(2,1)S(1)} %copy.217) | copy-start | bytes 3145732
  57.6 44.9 %all-to-all-start.1 = ((bf16[8,2,2048]{2,1,0:T(2,128)(2,1)}), bf16[8,2,2048]{2,1,0:T(2,128)(2,1)S(1)}, u32[]{:S(2)}, u32[]{:S(2)}) async-start(bf16[8,2,2048]{2,1,0:T(2,128)(2,1)} %reshape.474), calls=%async_computation.1 | async-start | bytes 131072 | tf_op jit(solution)/shard_map/all_to_all | solution.py:103
  101.9 5.5 copy-start.3
  168.5 1.0 copy-start.5
  169.4 1.8 copy-start.1
  173.6 12.2 %copy-start.2 = (bf16[2,9,64,8,64]{2,4,1,3,0:T(8,128)(2,1)S(1)}, bf16[2,9,64,8,64]{2,4,1,3,0:T(8,128)(2,1)}, u32[]{:S(2)}) copy-start(bf16[2,9,64,8,64]{2,4,1,3,0:T(8,128)(2,1)} %copy-done.1) | copy-start | bytes 3538948
  174.7 20.8 %all-to-all-start.2 = ((bf16[1,2,64,10,66]{4,1,3,0,2:T(2,128)(2,1)}), bf16[1,2,64,10,66]{4,1,3,0,2:T(2,128)(2,1)S(1)}, u32[]{:S(2)}, u32[]{:S(2)}) async-start(bf16[1,2,64,10,66]{4,1,3,0,2:T(2,128)(2,1)} %copy.255), calls=%async_computation.2 | async-start | bytes 655360 | tf_op jit(solution)/shard_map/all_to_all | solution.py:118
  181.8 277.8 %all-reduce.14.cloned.1.call-start = ((), (), s32[]{:S(2)}) async-start(), calls=%async_computation.6 | async-start | bytes 1703936 | tf_op jit(solution)/shard_map/psum | solution.py:136
  187.2 350.0 %all-gather.8.cloned.1.call-start = ((), (), s32[]{:S(2)}) async-start(), calls=%async_computation.5 | async-start | bytes 2129920 | tf_op jit(solution)/shard_map/all_gather | solution.py:130
  195.7 3.3 copy-start.4
  195.7 3.3 copy-start.11
  199.9 10.5 %all-to-all-start = ((bf16[2,128,128]{2,0,1:T(2,128)(2,1)}), bf16[2,128,128]{2,0,1:T(2,128)(2,1)S(1)}, u32[]{:S(2)}, u32[]{:S(2)}) async-start(bf16[2,128,128]{2,0,1:T(2,128)(2,1)} %copy.240), calls=%async_computation | async-start | bytes 131072 | tf_op jit(solution)/shard_map/all_to_all | solution.py:102
Sparse Core Ops, SparseCore 0:
  10.1 42.7 all-gather.3
  56.2 91.2 all-gather.5
  187.7 271.7 all-reduce.13
  462.6 74.5 all-gather.7
where the time goes:
time: 562 us; the launch traced here: 561 us
  waiting for transfers between devices  424 us (75%)
  local copies, waits for them, and re-layouts  54 us (10%)
  blocking collectives  39.5 us (7%)
  starting transfers between devices  15.2 us (3%)
  between operations  14.4 us (3%)
  other arithmetic  7.87 us (1%)
  matrix products  6.42 us (1%)
    psum x1, waiting for transfers between devices, shards(): conv_total, down_total = lax.psum((conv_part, down_part), ('space', 'chan'))  248 us
    all_gather x1, waiting for transfers between devices, shards(): lax.all_gather(rim_strips(grad_padded), 'space', axis=0, tiled=True)  74.2 us
    all_gather x1, waiting for transfers between devices, shards(): whole_features = lax.all_gather(features, 'chan', axis=1, tiled=True)  44.8 us
    all_gather x1, waiting for transfers between devices, shards(): gathered = lax.all_gather(edge_strips(images), 'space', axis=0, tiled=True)  40.1 us
    all_gather x1, blocking collectives, shards(): lax.all_gather(conv_weight, 'chan', axis=0, tiled=True)  20.6 us
    all_gather x1, blocking collectives, shards(): lax.all_gather(down_weight, 'chan', axis=0, tiled=True)  18.9 us
    all_gather x1, local copies, waits for them, and re-layouts, shards(): gathered = lax.all_gather(edge_strips(images), 'space', axis=0, tiled=True)  11.9 us
  transfers between devices with their start and end apart: 7, of which 6 were waited for; matrix products, arithmetic and copies ran while one was open for 4% of the time, Pallas kernels for 0%

commit v1 on v0

--- a/solution.py
+++ b/solution.py
@@ -127,7 +127,9 @@
     grad_padded = grad_padded.at[:, :, block_rows + 1 : tile_side + 2 : block_rows, :].add(
         stacked[:, :, :, block_rows + 1, :]
     )
-    rim_all = lax.all_gather(rim_strips(grad_padded), "space", axis=0, tiled=True)
+    x = rim_strips(grad_padded)
+    copies = jnp.concatenate([x] * lax.axis_size("space"), axis=0)
+    rim_all = lax.all_to_all(copies, "space", 0, 0, tiled=True)
     returned = bordering(rim_all, partner, orientation)
     features_grad = add_edges(grad_padded[:, :, 1:-1, 1:-1], returned).astype(jnp.bfloat16)
     features_grad = features_grad.reshape(tile_count, chan_part, tile_side * tile_side)

time: 562 us -> 528 us (0.940)
  waiting for transfers between devices: 424 us -> 374 us
  starting transfers between devices: 15.2 us -> 22.4 us
    all_gather x1 -> x0, waiting for transfers between devices: 74.2 us -> none  [shards(): lax.all_gather(rim_strips(grad_padded), 'space', axis=0, tiled=True)]
    psum x1, waiting for transfers between devices: 248 us -> 275 us  [shards(): conv_total, down_total = lax.psum((conv_part, down_part), ('space', 'chan'))]
    all_to_all x0 -> x1, starting transfers between devices: none -> 7.27 us  [shards(): rim_all = lax.all_to_all(copies, 'space', 0, 0, tiled=True)]
    all_to_all x1, waiting for transfers between devices: 7.15 us -> 0.64 us  [shards(): lax.all_to_all(pooled_band, 'chan', split_axis=1, concat_axis=2, tiled=True)]
  transfers between devices with their start and end apart: 7 -> 7, of which waited for: 6 -> 5; matrix products, arithmetic and copies ran while one was open for 4% -> 4% of each run, Pallas kernels for 0% -> 0%
where the time goes in v1:
time: 528 us; the launch traced here: 526 us
  waiting for transfers between devices  374 us (71%)
  local copies, waits for them, and re-layouts  58.5 us (11%)
  blocking collectives  39.9 us (8%)
  starting transfers between devices  22.4 us (4%)
  between operations  14.9 us (3%)
  other arithmetic  10.9 us (2%)
  matrix products  5.72 us (1%)
    psum x1, waiting for transfers between devices, shards(): conv_total, down_total = lax.psum((conv_part, down_part), ('space', 'chan'))  275 us
    all_gather x1, waiting for transfers between devices, shards(): whole_features = lax.all_gather(features, 'chan', axis=1, tiled=True)  44.9 us
    all_gather x1, waiting for transfers between devices, shards(): gathered = lax.all_gather(edge_strips(images), 'space', axis=0, tiled=True)  39.9 us
    all_gather x1, blocking collectives, shards(): lax.all_gather(conv_weight, 'chan', axis=0, tiled=True)  20.6 us
    all_gather x1, blocking collectives, shards(): lax.all_gather(down_weight, 'chan', axis=0, tiled=True)  19.3 us
    all_to_all x1, waiting for transfers between devices, shards(): lax.all_to_all(grad_block[None].astype(jnp.bfloat16), 'chan', split_axis=...  12.7 us
    all_gather x1, local copies, waits for them, and re-layouts, shards(): gathered = lax.all_gather(edge_strips(images), 'space', axis=0, tiled=True)  11.6 us
  transfers between devices with their start and end apart: 7, of which 5 were waited for; matrix products, arithmetic and copies ran while one was open for 4% of the time, Pallas kernels for 0%

profile of v1, /device:TPU:1, one launch (start us, length us, event | category | flops | bytes accessed | tf_op | source)
XLA Modules:
  0.0 526.5 jit_solution(17513769815015657285)
XLA Ops:
  8.0 44.9 %all-gather.3.cloned.1.call-done = bf16[2,64,4096]{2,1,0:T(8,128)(2,1)} async-done(((bf16[2,8,4096]{2,1,0:T(8,128)(2,1)}), bf16[2,64,4096]{2,1,0:T(8,128)(2,1)}) %all-gather.3.cloned.1.call-update) | async-done | bytes 1048592 | tf_op jit(solution)/shard_map/all_gather | solution.py:81
  52.8 2.0 copy.217
  57.6 4.4 all-to-all-start.1
  62.1 20.6 %all_gather.14 = bf16[128,9,64]{2,0,1:T(8,128)(2,1)S(1)} all-gather(bf16[16,9,64]{2,0,1:T(8,128)(2,1)S(1)} %copy-done.6), channel_id=1, replica_groups=mesh['space'=64,'chan'=8] {'chan'}, dimensions={0}, use_global_device_ids=true | all-gather | bytes 165888 | tf_op jit(solution)/shard_map/all_gather | solution.py:89
  82.7 19.3 %all_gather.15 = bf16[128,4,128]{2,1,0:T(4,128)(2,1)S(1)} all-gather(bf16[16,4,128]{2,1,0:T(4,128)(2,1)S(1)} %copy-done.7), channel_id=1, replica_groups=mesh['space'=64,'chan'=8] {'chan'}, dimensions={0}, use_global_device_ids=true | all-gather | bytes 147456 | tf_op jit(solution)/shard_map/all_gather | solution.py:90
  105.6 2.6 pad.68
  108.2 39.9 %all-gather.5.cloned.1.call-done = bf16[128,4,64,64]{2,3,0,1:T(8,128)(2,1)} async-done(((bf16[2,4,64,64]{2,3,0,1:T(8,128)(2,1)}), bf16[128,4,64,64]{2,3,0,1:T(8,128)(2,1)}) %all-gather.5.cloned.1.call-update) | async-done | bytes 4194320 | tf_op jit(solution)/shard_map/all_gather | solution.py:84
  148.1 11.6 %copy.224 = bf16[128,4,64,64]{3,2,1,0:T(8,128)(2,1)} copy(bf16[128,4,64,64]{2,3,0,1:T(8,128)(2,1)} %all-gather.5.cloned.1.call-done) | data formatting | bytes 8388608 | tf_op jit(solution)/shard_map/all_gather | solution.py:84
  159.7 4.0 gather_fusion
  164.2 1.5 scatter.14
  165.7 1.4 scatter.15
  174.6 7.1 %all-to-all-start.2 = ((bf16[1,2,64,10,66]{4,1,3,0,2:T(2,128)(2,1)}), bf16[1,2,64,10,66]{4,1,3,0,2:T(2,128)(2,1)S(1)}, u32[]{:S(2)}, u32[]{:S(2)}) async-start(bf16[1,2,64,10,66]{4,1,3,0,2:T(2,128)(2,1)} %copy.255), calls=%async_computation.2 | async-start | bytes 655360 | tf_op jit(solution)/shard_map/all_to_all | solution.py:118
  182.7 12.7 %all-to-all-done.2 = bf16[1,2,64,10,66]{4,1,3,0,2:T(2,128)(2,1)S(1)} async-done(((bf16[1,2,64,10,66]{4,1,3,0,2:T(2,128)(2,1)}), bf16[1,2,64,10,66]{4,1,3,0,2:T(2,128)(2,1)S(1)}, u32[]{:S(2)}, u32[]{:S(2)}) %all-to-all-start.2) | async-done | bytes 168992 | tf_op jit(solution)/shard_map/all_to_all | solution.py:118
  195.4 3.5 all-to-all-start
  202.9 2.3 reshape.476
  205.9 7.3 %all-to-all-start.3 = ((f32[64,1,4096]{2,1,0:T(1,128)}), f32[64,1,4096]{2,1,0:T(1,128)S(1)}, u32[]{:S(2)}, u32[]{:S(2)}) async-start(f32[64,1,4096]{2,1,0:T(1,128)} %reshape.476), calls=%async_computation.3 | async-start | bytes 2097152 | tf_op jit(solution)/shard_map/all_to_all | solution.py:132
  214.6 3.0 convolution_bitcast_fusion.1
  218.3 275.4 %all-reduce.14.cloned.1.call-done = (f32[128,9,64]{2,0,1:T(8,128)}, f32[128,4,128]{2,1,0:T(4,128)}) async-done(((f32[128,9,64]{2,0,1:T(8,128)}, f32[128,4,128]{2,1,0:T(4,128)}), (f32[128,9,64]{2,0,1:T(8,128)}, f32[128,4,128]{2,1,0:T(4,128)})) %all-reduce.14.cloned.1.call-update) | async-done | bytes 557072 | tf_op jit(solution)/shard_map/psum | solution.py:138
  495.1 1.5 dynamic-slice_multiply_fusion
  497.7 3.3 reduce.16
  500.9 2.2 reshape.477
  503.1 2.1 gather_fusion.1
  505.9 1.8 scatter-add.36
  508.3 10.4 %scatter-add.38 = f32[2,8,64,64]{2,1,0,3:T(8,128)S(1)} dynamic-update-slice(f32[2,8,64,64]{2,1,0,3:T(8,128)S(1)} %fusion.23, f32[2,8,1,64]{2,1,0,3:T(8,128)S(1)} %slice_add_fusion, s32[]{:T(128)} %constant.268.clone.1, s32[]{:T(128)} %constant.268.clone.1, s32[]{:T(128)} %constant.280.clone.1, s32[]{:T(128)} %constant.268.clone.1) | dynamic-update-slice | bytes 8196 | tf_op jit(solution)/shard_map/scatter-add | solution.py:42
  (178 shorter events, 26.9 us)
Async XLA Ops:
  7.2 45.7 %all-gather.3.cloned.1.call-start = ((), (), s32[]{:S(2)}) async-start(), calls=%async_computation.4 | async-start | bytes 1179648 | tf_op jit(solution)/shard_map/all_gather | solution.py:81
  7.9 48.1 %copy-start.5 = (bf16[2,16,1024]{2,1,0:T(8,128)(2,1)S(1)}, bf16[2,16,1024]{2,1,0:T(8,128)(2,1)}, u32[]{:S(2)}) copy-start(bf16[2,16,1024]{2,1,0:T(8,128)(2,1)} %param.25) | copy-start | bytes 196612
  7.9 54.1 %copy-start.8 = (s32[2,4]{1,0:T(2,128)S(1)}, s32[2,4]{1,0:T(2,128)}, u32[]{:S(2)}) copy-start(s32[2,4]{1,0:T(2,128)} %param.26) | copy-start | bytes 100
  7.9 54.1 %copy-start.6 = (bf16[16,9,64]{2,0,1:T(8,128)(2,1)S(1)}, bf16[16,9,64]{2,0,1:T(8,128)(2,1)}, u32[]{:S(2)}) copy-start(bf16[16,9,64]{2,0,1:T(8,128)(2,1)} %param.23) | copy-start | bytes 55300
  7.9 140.1 %all-gather.5.cloned.1.call-start = ((), (), s32[]{:S(2)}) async-start(), calls=%async_computation.5 | async-start | bytes 8519680 | tf_op jit(solution)/shard_map/all_gather | solution.py:84
  54.9 48.7 %copy-start = (bf16[2,64,4096]{1,2,0:T(8,128)(2,1)}, bf16[2,64,4096]{1,2,0:T(8,128)(2,1)S(1)}, u32[]{:S(2)}) copy-start(bf16[2,64,4096]{1,2,0:T(8,128)(2,1)S(1)} %copy.217) | copy-start | bytes 3145732
  54.9 27.8 %copy-start.9 = (s32[2,4]{1,0:T(2,128)S(1)}, s32[2,4]{1,0:T(2,128)}, u32[]{:S(2)}) copy-start(s32[2,4]{1,0:T(2,128)} %param.27) | copy-start | bytes 100
  54.9 27.8 %copy-start.7 = (bf16[16,4,128]{2,1,0:T(4,128)(2,1)S(1)}, bf16[16,4,128]{2,1,0:T(4,128)(2,1)}, u32[]{:S(2)}) copy-start(bf16[16,4,128]{2,1,0:T(4,128)(2,1)} %param.24) | copy-start | bytes 49156
  57.6 45.2 %all-to-all-start.1 = ((bf16[8,2,2048]{2,1,0:T(2,128)(2,1)}), bf16[8,2,2048]{2,1,0:T(2,128)(2,1)S(1)}, u32[]{:S(2)}, u32[]{:S(2)}) async-start(bf16[8,2,2048]{2,1,0:T(2,128)(2,1)} %reshape.474), calls=%async_computation.1 | async-start | bytes 131072 | tf_op jit(solution)/shard_map/all_to_all | solution.py:103
  103.7 0.7 copy-start.2
  168.8 1.0 copy-start.4
  169.6 1.4 copy-start.1
  171.1 10.6 %copy-start.10 = (bf16[2,128,8,64]{1,3,2,0:T(8,128)(2,1)}, bf16[2,128,8,64]{1,3,2,0:T(8,128)(2,1)S(1)}, u32[]{:S(2)}) copy-start(bf16[2,128,8,64]{1,3,2,0:T(8,128)(2,1)S(1)} %get-tuple-element.122) | copy-start | bytes 786436
  174.6 20.8 %all-to-all-start.2 = ((bf16[1,2,64,10,66]{4,1,3,0,2:T(2,128)(2,1)}), bf16[1,2,64,10,66]{4,1,3,0,2:T(2,128)(2,1)S(1)}, u32[]{:S(2)}, u32[]{:S(2)}) async-start(bf16[1,2,64,10,66]{4,1,3,0,2:T(2,128)(2,1)} %copy.255), calls=%async_computation.2 | async-start | bytes 655360 | tf_op jit(solution)/shard_map/all_to_all | solution.py:118
  195.4 10.5 %all-to-all-start = ((bf16[2,128,128]{2,0,1:T(2,128)(2,1)}), bf16[2,128,128]{2,0,1:T(2,128)(2,1)S(1)}, u32[]{:S(2)}, u32[]{:S(2)}) async-start(bf16[2,128,128]{2,0,1:T(2,128)(2,1)} %copy.240), calls=%async_computation | async-start | bytes 131072 | tf_op jit(solution)/shard_map/all_to_all | solution.py:102
  205.2 8.0 %copy-start.3 = (bf16[2,128,4,32]{3,2,1,0:T(4,128)(2,1)S(1)}, bf16[2,128,4,32]{3,2,1,0:T(4,128)(2,1)}, u32[]{:S(2)}) copy-start(bf16[2,128,4,32]{3,2,1,0:T(4,128)(2,1)} %copy-done.2) | copy-start | bytes 196612
  205.2 8.0 %copy-start.11 = (bf16[2,128,8,64]{1,3,2,0:T(8,128)(2,1)S(1)}, bf16[2,128,8,64]{1,3,2,0:T(8,128)(2,1)}, u32[]{:S(2)}) copy-start(bf16[2,128,8,64]{1,3,2,0:T(8,128)(2,1)} %copy-done.10) | copy-start | bytes 786436
  205.9 291.3 %all-to-all-start.3 = ((f32[64,1,4096]{2,1,0:T(1,128)}), f32[64,1,4096]{2,1,0:T(1,128)S(1)}, u32[]{:S(2)}, u32[]{:S(2)}) async-start(f32[64,1,4096]{2,1,0:T(1,128)} %reshape.476), calls=%async_computation.3 | async-start | bytes 2097152 | tf_op jit(solution)/shard_map/all_to_all | solution.py:132
  213.2 280.6 %all-reduce.14.cloned.1.call-start = ((), (), s32[]{:S(2)}) async-start(), calls=%async_computation.6 | async-start | bytes 1703936 | tf_op jit(solution)/shard_map/psum | solution.py:138
Sparse Core Ops, SparseCore 0:
  10.1 42.7 all-gather.2
  56.8 91.2 all-gather.4
  219.1 274.5 all-reduce.13
